TPU v7x, 32 devices: a whole 2x2x4 slice. The times are simulated.
32 devices in a mesh: req: 8 (over y, x, core), head: 4 (over z).
Axes of the slice: x: 2, y: 2, z: 4, core: 2. Of those that a mesh axis runs over, the one named last changes fastest.
Arguments:
- tokens: bfloat16 [4096, 2048], P('req'), may hold values from -6 to 6
- norm_gain: float32 [2048], replicated, may hold values from 0.1 to 1.9
- router_weight: float32 [2048, 8], replicated, may hold values from -0.125 to 0.125
- kv_weight: bfloat16 [2048, 4096], P('req', 'head'), may hold values from -0.125 to 0.125
- query_weight: bfloat16 [8, 2048, 2048], P(None, 'req', 'head'), may hold values from -0.125 to 0.125
- out_weight: bfloat16 [8, 2048, 2048], P(None, 'head', 'req'), may hold values from -0.5 to 0.5
- expert_ids: int32 [4096, 2], P('req'), may hold values from 0 to 7, all different within a row
- lengths: int32 [8], replicated, may hold values from 128 to 2048, as said below
- kv_cache: bfloat16 [8, 16, 2048, 256], P('req', 'head'), may hold values from -320 to 320
Outputs:
- attended: bfloat16 [4096, 2048], P(('req', 'head'))
- new_kv: bfloat16 [8, 16, 512, 256], P('req', 'head')
Inputs may be any that keep to these rules, and one draw needn't show every extreme that they name: `lengths`: some request holds exactly 2048 cached positions.
All inputs are finite; a program needn't handle non-finite values.
Results may differ from a plain program's by a relative error of at most 0.012.
The roundings to bfloat16 on the way count: a program that leaves them out, or rounds other values in their place, can miss the bound.
Values may be sent and summed in bfloat16 or wider, within the bound.
No kernel may reach another device: no remote copies, remote signals or barrier semaphores. Data moves between devices by JAX's collectives and lax.ppermute only.
A program may use at most 128 MiB of HBM per device.

v0:
```python
import math
import jax
import jax.numpy as jnp
from jax import lax
from jax.sharding import PartitionSpec as P

NEG_LARGE = -1e30
EPSILON = 1e-06


def normalize(tokens, norm_gain):
    widened = tokens.astype(jnp.float32)
    factor = lax.rsqrt(jnp.mean(widened * widened, axis=-1, keepdims=True) + EPSILON)
    return (widened * factor * norm_gain).astype(jnp.bfloat16)


def gate_pair(normed, router_weight, expert_ids):
    logits = jnp.dot(normed.astype(jnp.float32), router_weight, precision=lax.Precision.HIGHEST)
    one_hot = jnp.arange(router_weight.shape[1])[None, None, :] == expert_ids[:, :, None]
    chosen = jnp.sum(jnp.where(one_hot, logits[:, None, :], 0.0), axis=-1)
    logit_gap = chosen[:, 1] - chosen[:, 0]
    return jnp.stack([1.0 / (1.0 + jnp.exp(logit_gap)), 1.0 / (1.0 + jnp.exp(-logit_gap))], axis=1)


def rotate(vectors, positions):
    half_dim = vectors.shape[-1] // 2
    inv_freq = jnp.exp(-math.log(10000.0) * jnp.arange(half_dim, dtype=jnp.float32) / half_dim)
    angles = positions[:, None] * inv_freq[None, :]
    cosine_table = jnp.cos(angles)
    sine_table = jnp.sin(angles)
    front_half = vectors[..., :half_dim]
    back_half = vectors[..., half_dim:]
    return jnp.concatenate(
        [
            front_half * cosine_table - back_half * sine_table,
            back_half * cosine_table + front_half * sine_table,
        ],
        axis=-1,
    )


def pick_length(lengths, wanted):
    return jnp.sum(jnp.where(jnp.arange(lengths.shape[0]) == wanted, lengths, 0))


def absorb(carry_state, queries, key_rows, value_rows, allowed):
    row_peak, row_total, row_accum = carry_state
    scale_factor = queries.shape[-1] ** (-0.5)
    scores = (
        jnp.einsum("hqd,hkd->hqk", queries, key_rows, preferred_element_type=jnp.float32)
        * scale_factor
    )
    scores = jnp.where(allowed[None], scores, NEG_LARGE)
    new_peak = jnp.maximum(row_peak, jnp.max(scores, axis=-1))
    weights = jnp.where(allowed[None], jnp.exp(scores - new_peak[..., None]), 0.0)
    shrink = jnp.exp(row_peak - new_peak)
    row_total = row_total * shrink + jnp.sum(weights, axis=-1)
    row_accum = row_accum * shrink[..., None] + jnp.einsum(
        "hqk,hkd->hqd", weights.astype(jnp.bfloat16), value_rows, preferred_element_type=jnp.float32
    )
    return (new_peak, row_total, row_accum)


def cache_pass(
    queries, source, lowest, highest, first_block, last_block, anchor, block_len, carry_state
):
    head_dim = source.shape[2] // 2

    def block_step(block_id, running):
        block_rows = lax.dynamic_slice_in_dim(source, block_id * block_len, block_len, 1)
        key_index = anchor + block_id * block_len + jnp.arange(block_len)
        allowed = ((key_index >= lowest) & (key_index < highest))[None, :]
        return absorb(
            running, queries, block_rows[..., :head_dim], block_rows[..., head_dim:], allowed
        )

    return lax.fori_loop(
        jnp.asarray(first_block, jnp.int32),
        jnp.asarray(last_block, jnp.int32),
        block_step,
        carry_state,
    )


def chain_reduce(parts, axis):
    count = lax.axis_size(axis)
    me = lax.axis_index(axis)
    blocks = parts.reshape(count, parts.shape[0] // count, parts.shape[1])
    own = lax.dynamic_index_in_dim(blocks, me, 0, keepdims=False).astype(jnp.float32)
    if count == 1:
        return own.astype(parts.dtype)

    def run(step_block, pairs_of):
        received = None
        for step in range(1, count):
            block = lax.dynamic_index_in_dim(
                blocks, jnp.clip(step_block(step), 0, count - 1), 0, keepdims=False
            )
            if received is not None:
                block = (received.astype(jnp.float32) + block.astype(jnp.float32)).astype(
                    parts.dtype
                )
            received = lax.ppermute(block, axis, pairs_of(step))
        return received.astype(jnp.float32)

    rightward = run(
        lambda step: me + count - step,
        lambda step: [(src, src + 1) for src in range(step) if src + 1 < count],
    )
    leftward = run(
        lambda step: me - count + step,
        lambda step: [(src, src - 1) for src in range(count - step, count) if src >= 1],
    )
    return (own + rightward + leftward).astype(parts.dtype)


def exchange_reduce(rows, weight, axis):
    count = lax.axis_size(axis)
    me = lax.axis_index(axis)
    span = rows.shape[0] // count
    total = None
    for shift in list(range(1, count)) + [0]:
        target = lax.rem(me + shift, count)
        block_rows = lax.dynamic_slice_in_dim(rows, target * span, span, 0)
        part = jnp.dot(block_rows, weight, preferred_element_type=jnp.float32).astype(jnp.bfloat16)
        if shift:
            part = lax.ppermute(part, axis, [(src, (src + shift) % count) for src in range(count)])
        part = part.astype(jnp.float32)
        total = part if total is None else total + part
    return total.astype(jnp.bfloat16)


def shards(
    tokens,
    norm_gain,
    router_weight,
    kv_weight,
    query_weight,
    out_weight,
    expert_ids,
    lengths,
    kv_cache,
):
    normed = normalize(tokens, norm_gain)
    tok_count = normed.shape[0]
    experts = query_weight.shape[0]
    head_dim = kv_cache.shape[3] // 2
    local_heads = query_weight.shape[2] // head_dim
    cache_len = kv_cache.shape[2]
    block_len = min(512, cache_len // 4)
    gate_values = gate_pair(normed, router_weight, expert_ids)
    query_full = lax.all_gather(query_weight, "req", axis=1, tiled=True)
    query_full, kv_weight, out_weight = lax.optimization_barrier(
        (query_full, kv_weight, out_weight)
    )
    kv_full = lax.all_gather(kv_weight, "req", axis=0, tiled=True)
    out_full = lax.all_gather(out_weight, "req", axis=2, tiled=True)
    projected = jnp.dot(normed, kv_full, preferred_element_type=jnp.float32)
    query_all = jnp.einsum("tc,ecn->ten", normed, query_full, preferred_element_type=jnp.float32)
    req_index = lax.axis_index("req")
    own_length = pick_length(lengths, req_index)
    positions = (own_length + jnp.arange(tok_count)).astype(jnp.float32)
    projected = projected.reshape(tok_count, local_heads, 2, head_dim)
    new_keys = rotate(jnp.transpose(projected[:, :, 0], (1, 0, 2)), positions)
    new_values = jnp.transpose(projected[:, :, 1], (1, 0, 2))
    fresh_kv = jnp.concatenate([new_keys, new_values], axis=-1).astype(jnp.bfloat16)
    one_hot = jnp.arange(experts)[None, None, :] == expert_ids[:, :, None]
    query_sel = jnp.sum(jnp.where(one_hot[..., None], query_all[:, None], 0.0), axis=2)
    queries = jnp.transpose(query_sel.reshape(tok_count * 2, local_heads, head_dim), (1, 0, 2))
    queries = rotate(queries, jnp.repeat(positions, 2)).astype(jnp.bfloat16)
    own_cache = kv_cache[0]
    query_rows = tok_count * 2
    empty_state = (
        jnp.full((local_heads, query_rows), NEG_LARGE, jnp.float32),
        jnp.zeros((local_heads, query_rows), jnp.float32),
        jnp.zeros((local_heads, query_rows, head_dim), jnp.float32),
    )
    carry_state = cache_pass(
        queries,
        own_cache,
        0,
        own_length,
        0,
        (own_length + block_len - 1) // block_len,
        0,
        block_len,
        empty_state,
    )
    row_ids = jnp.arange(query_rows) // 2
    causal = row_ids[:, None] >= jnp.arange(tok_count)[None, :]
    carry_state = absorb(
        carry_state, queries, fresh_kv[..., :head_dim], fresh_kv[..., head_dim:], causal
    )
    heads_out = carry_state[2] / carry_state[1][..., None]
    heads_out = jnp.transpose(heads_out, (1, 0, 2)).reshape(tok_count, 2, local_heads * head_dim)
    weighted = (gate_values[:, :, None] * heads_out).astype(jnp.bfloat16)
    mixture = jnp.sum(jnp.where(one_hot[..., None], weighted[:, :, None, :], 0), axis=1)
    mixture_flat = mixture.reshape(tok_count, experts * local_heads * head_dim)
    flat_piece = out_full.reshape(experts * local_heads * head_dim, out_full.shape[2])
    result = exchange_reduce(mixture_flat, flat_piece, "head")
    return (result, fresh_kv[None])


def solution(mesh):
    placed = (
        P("req", None),
        P(),
        P(),
        P("req", "head"),
        P(None, "req", "head"),
        P(None, "head", "req"),
        P("req", None),
        P(),
        P("req", "head", None, None),
    )
    return jax.shard_map(
        shards,
        mesh=mesh,
        in_specs=placed,
        out_specs=(P(("req", "head"), None), P("req", "head", None, None)),
        check_vma=False,
    )
```

profile of v0, /device:TPU:9, one launch (start us, length us, event | category | flops | bytes accessed | tf_op | source)
XLA Modules:
  0.0 309.7 jit_solution(12866438923315046674)
XLA Ops:
  8.0 93.4 %all-gather.4.cloned.1.call-done = bf16[8,2048,512]{2,1,0:T(8,128)(2,1)} async-done(((bf16[8,256,512]{2,1,0:T(8,128)(2,1)}), bf16[8,2048,512]{2,1,0:T(8,128)(2,1)}) %all-gather.4.cloned.1.call-update) | async-done | bytes 16777232 | tf_op jit(solution)/shard_map/all_gather | solution.py:152
  108.4 2.0 multiply_cosine_fusion.1
  111.5 1.9 multiply_cosine_fusion
  113.4 11.9 %fusion.31 = f32[512,8,512]{2,0,1:T(8,128)S(1)} fusion(bf16[8,2048,512]{2,1,0:T(8,128)(2,1)} %all-gather.4.cloned.1.call-done, bf16[512,2048]{1,0:T(8,128)(2,1)S(1)} %copy-done.8, f32[2048]{0:T(1024)S(1)} %copy-done.14, f32[512]{0:T(512)S(1)} %add_rsqrt_fusion), kind=kOutput, calls=%fused_computation.44 | convolution fusion | flops 8594128896 | bytes 27273216 | tf_op jit(solution)/shard_map/tc,ecn->ten/dot_general | solution.py:159
  125.2 4.9 %copy.40 = f32[512,8,512]{2,1,0:T(8,128)S(1)} copy(f32[512,8,512]{2,0,1:T(8,128)S(1)} %fusion.31) | data formatting | bytes 16777216 | tf_op jit(solution)/shard_map/tc,ecn->ten/dot_general | solution.py:159
  130.1 8.2 %select_reduce_fusion = f32[512,2,512]{2,1,0:T(2,128)} fusion(f32[512,8,512]{2,1,0:T(8,128)S(1)} %copy.40, pred[512,2,8]{2,1,0:T(4,128)(4,1)S(1)} %copy.38), kind=kLoop, calls=%fused_computation.25 | loop fusion | flops 7864320 | bytes 10493952 | tf_op jit(solution)/shard_map/reduce_sum | solution.py:168
  138.3 3.4 %reshape.253 = f32[1024,4,128]{2,1,0:T(4,128)S(1)} reshape(f32[512,2,512]{2,1,0:T(2,128)} %select_reduce_fusion) | data formatting | bytes 4194304 | tf_op jit(solution)/shard_map/reshape | solution.py:169
  144.7 31.4 %while.14 = (s32[]{:T(128)}, f32[4,1024]{1,0:T(4,128)S(1)}, f32[4,1024]{1,0:T(4,128)S(1)}, f32[4,1024,128]{2,1,0:T(8,128)}, s32[]{:T(128)}, /*index=5*/s32[]{:T(...) while((s32[]{:T(128)}, f32[4,1024]{1,0:T(4,128)S(1)}, ...), condition=%wide.region_7.8_spmd, body=%wide.region_4.7_spmd.sunk | while | flops 1102063616 | bytes 65276644 | solution.py:77
  145.6 2.4 bitcast_reduce_fusion.2
  148.0 2.5 fusion.82
  152.2 9.0 %multiply_add_fusion.6 = f32[4,1024,128]{2,1,0:T(8,128)} fusion(f32[4,1024,128]{2,1,0:T(8,128)} %get-tuple-element.164, f32[4,512,1024]{2,1,0:T(8,128)} %copy-done.2, f32[4,1024]{1,0:T(4,128)S(1)} %max.8, pred[512]{0:T(512)(128)(4,1)S(1)} %fusion.81, f32[4,1024]{1,0:T(4,128)S(1)} %get-tuple-element.147, ...), kind=kOutput, calls=%fused_computation.10.clone.1 | convolution fusion | flops 548405248 | bytes 13141000 | tf_op jit(solution)/shard_map/while/body/hqk,hkd->hqd/dot_general | solution.py:58
  161.8 2.4 bitcast_reduce_fusion.2
  164.3 2.5 fusion.82
  167.5 8.5 %multiply_add_fusion.6 = f32[4,1024,128]{2,1,0:T(8,128)} fusion(f32[4,1024,128]{2,1,0:T(8,128)} %get-tuple-element.164, f32[4,512,1024]{2,1,0:T(8,128)} %copy-done.2, f32[4,1024]{1,0:T(4,128)S(1)} %max.8, pred[512]{0:T(512)(128)(4,1)S(1)} %fusion.81, f32[4,1024]{1,0:T(4,128)S(1)} %get-tuple-element.147, ...), kind=kOutput, calls=%fused_computation.10.clone.1 | convolution fusion | flops 548405248 | bytes 13141000 | tf_op jit(solution)/shard_map/while/body/hqk,hkd->hqd/dot_general | solution.py:58
  176.1 5.9 %fusion.59 = f32[512,1024]{1,0:T(8,128)} fusion(bf16[2048,1024]{1,0:T(8,128)(2,1)} %all-gather.6.cloned.1.call-done, bf16[512,2048]{1,0:T(8,128)(2,1)S(1)} %copy-done.9, f32[2048]{0:T(1024)S(1)} %copy-done.14, f32[512]{0:T(512)S(1)} %add_rsqrt_fusion), kind=kOutput, calls=%fused_computation.101 | convolution fusion | flops 2151677952 | bytes 8398848 | tf_op jit(solution)/shard_map/dot_general | solution.py:158
  181.9 3.7 %reshape.254 = f32[512,4,2,128]{3,2,1,0:T(2,128)S(1)} reshape(f32[512,1024]{1,0:T(8,128)} %fusion.59) | data formatting | bytes 4194304 | tf_op jit(solution)/shard_map/reshape | solution.py:163
  188.1 1.9 fusion.21
  190.0 2.1 fusion.22
  192.2 4.0 %divide_bitcast_fusion = f32[1024,4,128]{2,0,1:T(8,128)S(1)} fusion(f32[4,1024,128]{2,1,0:T(8,128)S(1)} %copy-done.10, f32[4,1024,512]{1,2,0:T(8,128)S(1)} %get-tuple-element.89, f32[4,1024]{1,0:T(4,128)S(1)} %max.6, pred[1024,512]{0,1:T(8,128)(4,1)S(1)} %copy-done.5, f32[4,1024]{1,0:T(4,128)S(1)} %get-tuple-element.76, ...), kind=kOutput, calls=%fused_computation.48 | convolution fusion | flops 548929536 | bytes 13680640 | tf_op jit(solution)/shard_map/hqk,hkd->hqd/dot_general | solution.py:58
  196.2 2.7 copy.45
  198.9 3.0 reshape.255
  201.8 1.9 multiply_convert_fusion
  203.7 7.2 %select_reduce_fusion.1 = bf16[512,8,512]{2,1,0:T(8,128)(2,1)S(1)} fusion(pred[512,2,8]{2,1,0:T(4,128)(4,1)S(1)} %copy.38, bf16[512,2,512]{2,1,0:T(2,128)(2,1)S(1)} %multiply_convert_fusion), kind=kLoop, calls=%fused_computation.26 | loop fusion | flops 6291456 | bytes 5251072 | tf_op jit(solution)/shard_map/reduce_sum | solution.py:197
  210.9 4.2 %copy.50 = bf16[64,8,8,512]{3,1,2,0:T(8,128)(2,1)} copy(bf16[64,8,8,512]{3,2,1,0:T(8,128)(2,1)S(1)} %bitcast.64) | data formatting | bytes 8388608
  215.1 20.0 %all-gather.8.cloned.1.call-done = bf16[8,512,2048]{2,1,0:T(8,128)(2,1)} async-done(((bf16[8,512,256]{2,1,0:T(8,128)(2,1)}), bf16[8,512,2048]{2,1,0:T(8,128)(2,1)}) %all-gather.8.cloned.1.call-update) | async-done | bytes 16777232 | tf_op jit(solution)/shard_map/all_gather | solution.py:157
  235.1 9.4 %convolution_convert_fusion.3 = bf16[128,2048]{1,0:T(8,128)(2,1)} fusion(bf16[4096,2048]{1,0:T(8,128)(2,1)} %bitcast.59, bf16[512,4096]{1,0:T(8,128)(2,1)} %bitcast.65, s32[]{:T(128)S(6)} %select_n.72), kind=kOutput, calls=%fused_computation.43 | convolution fusion | flops 2147745792 | bytes 18350084 | tf_op jit(solution)/shard_map/dot_general | solution.py:125
  247.4 3.3 %convolution_convert_fusion.2 = bf16[128,2048]{1,0:T(8,128)(2,1)} fusion(bf16[4096,2048]{1,0:T(8,128)(2,1)S(1)} %bitcast.61, bf16[512,4096]{1,0:T(8,128)(2,1)S(1)} %bitcast.67, s32[]{:T(128)S(6)} %select_n.73), kind=kOutput, calls=%fused_computation.42 | convolution fusion | flops 2147745792 | bytes 18350084 | tf_op jit(solution)/shard_map/dot_general | solution.py:125
  250.7 2.1 collective-permute-start.1
  252.8 3.3 %convolution_convert_fusion.1 = bf16[128,2048]{1,0:T(8,128)(2,1)} fusion(bf16[4096,2048]{1,0:T(8,128)(2,1)S(1)} %bitcast.62, bf16[512,4096]{1,0:T(8,128)(2,1)S(1)} %bitcast.68, s32[]{:T(128)S(6)} %select_n.74), kind=kOutput, calls=%fused_computation.41 | convolution fusion | flops 2147745792 | bytes 18350084 | tf_op jit(solution)/shard_map/dot_general | solution.py:125
  258.2 32.8 %collective-permute-done.1 = bf16[128,2048]{1,0:T(8,128)(2,1)} collective-permute-done((bf16[128,2048]{1,0:T(8,128)(2,1)}, bf16[128,2048]{1,0:T(8,128)(2,1)}, u32[]{:S(2)}, u32[]{:S(2)}) %collective-permute-start.1) | collective-permute-done | bytes 524320 | tf_op jit(solution)/shard_map/ppermute | solution.py:127
  291.0 2.5 collective-permute-done.2
  293.5 9.5 %add_convert_fusion.1 = bf16[128,2048]{1,0:T(8,128)(2,1)} fusion(bf16[128,2048]{1,0:T(8,128)(2,1)} %collective-permute-done.2, bf16[128,2048]{1,0:T(8,128)(2,1)} %collective-permute-done.1, bf16[128,2048]{1,0:T(8,128)(2,1)S(1)} %collective-permute-done, bf16[4096,2048]{1,0:T(8,128)(2,1)} %bitcast.60, bf16[512,4096]{1,0:T(8,128)(2,1)} %bitcast.66, ...), kind=kOutput, calls=%fused_computation.56 | convolution fusion | flops 2149842944 | bytes 19922948 | tf_op jit(solution)/shard_map/dot_general | solution.py:125
  (83 shorter events, 22.2 us)
Async XLA Ops:
  7.2 98.4 %copy-start = (f32[2048,8]{0,1:T(8,128)S(1)}, f32[2048,8]{0,1:T(8,128)}, u32[]{:S(2)}) copy-start(f32[2048,8]{0,1:T(8,128)} %param.13) | copy-start | bytes 196612
  7.2 95.0 %copy-start.15 = (s32[8]{0:T(128)S(1)}, s32[8]{0:T(128)}, u32[]{:S(2)}) copy-start(s32[8]{0:T(128)} %param.18) | copy-start | bytes 100
  7.2 97.4 %copy-start.13 = (s32[512,2]{0,1:T(2,128)S(1)}, s32[512,2]{0,1:T(2,128)}, u32[]{:S(2)}) copy-start(s32[512,2]{0,1:T(2,128)} %param.17) | copy-start | bytes 12292
  7.2 97.9 %copy-start.8 = (bf16[512,2048]{1,0:T(8,128)(2,1)S(1)}, bf16[512,2048]{1,0:T(8,128)(2,1)}, u32[]{:S(2)}) copy-start(bf16[512,2048]{1,0:T(8,128)(2,1)} %param.11) | copy-start | bytes 6291460
  7.2 98.4 %copy-start.14 = (f32[2048]{0:T(1024)S(1)}, f32[2048]{0:T(1024)}, u32[]{:S(2)}) copy-start(f32[2048]{0:T(1024)} %param.12) | copy-start | bytes 24580
  7.2 94.2 %all-gather.4.cloned.1.call-start = ((), (), s32[]{:S(2)}) async-start(), calls=%async_computation | async-start | bytes 18874368 | tf_op jit(solution)/shard_map/all_gather | solution.py:152
  8.0 168.1 %all-gather.6.cloned.1.call-start = ((), (), s32[]{:S(2)}) async-start(), calls=%async_computation.1 | async-start | bytes 4718592 | tf_op jit(solution)/shard_map/all_gather | solution.py:156
  101.5 133.6 %all-gather.8.cloned.1.call-start = ((), (), s32[]{:S(2)}) async-start(), calls=%async_computation.2 | async-start | bytes 18874368 | tf_op jit(solution)/shard_map/all_gather | solution.py:157
  144.7 31.4 %copy-start.9 = (bf16[512,2048]{1,0:T(8,128)(2,1)S(1)}, bf16[512,2048]{1,0:T(8,128)(2,1)}, u32[]{:S(2)}) copy-start(bf16[512,2048]{1,0:T(8,128)(2,1)} %param.11) | copy-start | bytes 6291460
  148.0 4.2 %copy-start.2 = (f32[4,512,1024]{2,1,0:T(8,128)}, f32[4,512,1024]{2,1,0:T(8,128)S(1)}, u32[]{:S(2)}) copy-start(f32[4,512,1024]{2,1,0:T(8,128)S(1)} %get-tuple-element.145) | copy-start | bytes 25165828 | tf_op jit(solution)/shard_map/while
  164.3 3.2 %copy-start.2 = (f32[4,512,1024]{2,1,0:T(8,128)}, f32[4,512,1024]{2,1,0:T(8,128)S(1)}, u32[]{:S(2)}) copy-start(f32[4,512,1024]{2,1,0:T(8,128)S(1)} %get-tuple-element.145) | copy-start | bytes 25165828 | tf_op jit(solution)/shard_map/while
  185.7 1.9 copy-start.11
  185.7 1.9 copy-start.12
  186.4 1.7 copy-start.5
  187.5 4.7 %copy-start.6 = (bf16[512,4,1,128]{3,2,1,0:T(2,128)(2,1)}, bf16[512,4,1,128]{3,2,1,0:T(2,128)(2,1)S(1)}, u32[]{:S(2)}) copy-start(bf16[512,4,1,128]{3,2,1,0:T(2,128)(2,1)S(1)} %slice.53) | copy-start | bytes 1572868
  190.0 2.2 copy-start.10
  235.1 11.0 %copy-start.3 = (bf16[8,512,2048]{2,1,0:T(8,128)(2,1)S(1)}, bf16[8,512,2048]{2,1,0:T(8,128)(2,1)}, u32[]{:S(2)}) copy-start(bf16[8,512,2048]{2,1,0:T(8,128)(2,1)} %all-gather.8.cloned.1.call-done) | copy-start | bytes 50331652
  235.1 12.2 %copy-start.4 = (bf16[64,8,8,512]{3,1,2,0:T(8,128)(2,1)S(1)}, bf16[64,8,8,512]{3,1,2,0:T(8,128)(2,1)}, u32[]{:S(2)}) copy-start(bf16[64,8,8,512]{3,1,2,0:T(8,128)(2,1)} %copy.50) | copy-start | bytes 12582916
  244.5 13.7 %collective-permute-start = (bf16[128,2048]{1,0:T(8,128)(2,1)}, bf16[128,2048]{1,0:T(8,128)(2,1)S(1)}, u32[]{:S(2)}, u32[]{:S(2)}) collective-permute-start(bf16[128,2048]{1,0:T(8,128)(2,1)} %convolution_convert_fusion.3), channel_id=1, source_target_pairs={{0,1},{1,2},{2,3},{3,0},{4,5},{5,6},{6,7},{7,4},{8,9},{9,10},{10,1... | collective-permute-start | bytes 1572872 | tf_op jit(solution)/shard_map/ppermute | solution.py:127
  250.7 5.7 %copy-start.7 = (bf16[512,4,1,128]{3,2,1,0:T(2,128)(2,1)S(1)}, bf16[512,4,1,128]{3,2,1,0:T(2,128)(2,1)}, u32[]{:S(2)}) copy-start(bf16[512,4,1,128]{3,2,1,0:T(2,128)(2,1)} %copy-done.6) | copy-start | bytes 1572868
  250.7 40.3 %collective-permute-start.1 = (bf16[128,2048]{1,0:T(8,128)(2,1)}, bf16[128,2048]{1,0:T(8,128)(2,1)}, u32[]{:S(2)}, u32[]{:S(2)}) collective-permute-start(bf16[128,2048]{1,0:T(8,128)(2,1)} %convolution_convert_fusion.2), channel_id=1, source_target_pairs={{0,2},{1,3},{2,0},{3,1},{4,6},{5,7},{6,4},{7,5},{8,10},{9,11},{10,... | collective-permute-start | bytes 1572872 | tf_op jit(solution)/shard_map/ppermute | solution.py:127
  256.1 37.4 %collective-permute-start.2 = (bf16[128,2048]{1,0:T(8,128)(2,1)}, bf16[128,2048]{1,0:T(8,128)(2,1)}, u32[]{:S(2)}, u32[]{:S(2)}) collective-permute-start(bf16[128,2048]{1,0:T(8,128)(2,1)} %convolution_convert_fusion.1), channel_id=1, source_target_pairs={{0,3},{1,0},{2,1},{3,2},{4,7},{5,4},{6,5},{7,6},{8,11},{9,8},{10,9... | collective-permute-start | bytes 1572872 | tf_op jit(solution)/shard_map/ppermute | solution.py:127
  293.4 9.5 %copy-start.1 = (f32[2048,8]{0,1:T(8,128)S(1)}, f32[2048,8]{0,1:T(8,128)}, u32[]{:S(2)}) copy-start(f32[2048,8]{0,1:T(8,128)} %param.13) | copy-start | bytes 196612
Sparse Core Ops, SparseCore 0:
  10.0 91.4 all-gather.3
  103.3 36.7 all-gather.5
  142.0 93.1 all-gather.7
where the time goes:
time: 313 us; the launch traced here: 310 us
  waiting for transfers between devices  150 us (48%)
  matrix products  73.2 us (23%)
  other arithmetic  36.2 us (12%)
  local copies, waits for them, and re-layouts  30.8 us (10%)
  between operations  15.1 us (5%)
  starting transfers between devices  3.91 us (1%)
    all_gather x1, waiting for transfers between devices, shards(): query_full = lax.all_gather(query_weight, 'req', axis=1, tiled=True)  93.4 us
    ppermute x3, waiting for transfers between devices, exchange_reduce(): lax.ppermute(part, axis, [(src, (src + shift) % count) for src in range(c...  35.6 us
    dot_general x4, matrix products, exchange_reduce(): jnp.dot(block_rows, weight, preferred_element_type=jnp.float32)  25.5 us
    dot_general x3, matrix products, absorb(): jnp.einsum('hqk,hkd->hqd', weights.astype(jnp.bfloat16), value_rows, pref...  21.5 us
    all_gather x1, waiting for transfers between devices, shards(): out_full = lax.all_gather(out_weight, 'req', axis=2, tiled=True)  20 us
    dot_general x1, matrix products, shards(): jnp.einsum('tc,ecn->ten', normed, query_full, preferred_element_type=jnp....  11.9 us
    reduce_sum x1, other arithmetic, shards(): jnp.sum(jnp.where(one_hot[..., None], query_all[:, None], 0.0), axis=2)  8.24 us
    reduce_sum x1, other arithmetic, shards(): jnp.sum(jnp.where(one_hot[..., None], weighted[:, :, None, :], 0), axis=1)  7.15 us
  transfers between devices with their start and end apart: 6, of which 5 were waited for; matrix products, arithmetic and copies ran while one was open for 38% of the time, Pallas kernels for 0%

commit v1 on v0

--- a/solution.py
+++ b/solution.py
@@ -6,6 +6,18 @@
 
 NEG_LARGE = -1e30
 EPSILON = 1e-06
+
+
+def gather_by_bits(x, axis, dim):
+    ways, here = (lax.axis_size(axis), lax.axis_index(axis))
+    grown, reach = (x, 1)
+    while reach < ways:
+        theirs = lax.ppermute(grown, axis, [(d, d ^ reach) for d in range(ways)])
+        mine_first = jnp.concatenate([grown, theirs], axis=dim)
+        theirs_first = jnp.concatenate([theirs, grown], axis=dim)
+        grown = jnp.where(here & reach == 0, mine_first, theirs_first)
+        reach = 2 * reach
+    return grown
 
 
 def normalize(tokens, norm_gain):
@@ -149,7 +161,7 @@
     cache_len = kv_cache.shape[2]
     block_len = min(512, cache_len // 4)
     gate_values = gate_pair(normed, router_weight, expert_ids)
-    query_full = lax.all_gather(query_weight, "req", axis=1, tiled=True)
+    query_full = gather_by_bits(query_weight, "req", 1)
     query_full, kv_weight, out_weight = lax.optimization_barrier(
         (query_full, kv_weight, out_weight)
     )

time: 313 us -> 535 us (1.71)
  waiting for transfers between devices: 150 us -> 333 us
  other arithmetic: 36.2 us -> 71.4 us
    ppermute x0 -> x3, waiting for transfers between devices: none -> 275 us  [gather_by_bits(): theirs = lax.ppermute(grown, axis, [(d, d ^ reach) for d in range(ways)])]
    all_gather x1 -> x0, waiting for transfers between devices: 93.4 us -> none  [shards(): query_full = lax.all_gather(query_weight, 'req', axis=1, tiled=True)]
    select_n x0 -> x3, other arithmetic: none -> 35.2 us  [gather_by_bits(): grown = jnp.where(here & reach == 0, mine_first, theirs_first)]
  transfers between devices with their start and end apart: 6 -> 8, of which waited for: 5 -> 7; matrix products, arithmetic and copies ran while one was open for 38% -> 22% of each run, Pallas kernels for 0% -> 0%
where the time goes in v1:
time: 535 us; the launch traced here: 530 us
  waiting for transfers between devices  333 us (62%)
  matrix products  73.5 us (14%)
  other arithmetic  71.4 us (13%)
  local copies, waits for them, and re-layouts  30.1 us (6%)
  between operations  15.4 us (3%)
  starting transfers between devices  7.05 us (1%)
    ppermute x3, waiting for transfers between devices, gather_by_bits(): theirs = lax.ppermute(grown, axis, [(d, d ^ reach) for d in range(ways)])  275 us
    ppermute x3, waiting for transfers between devices, exchange_reduce(): lax.ppermute(part, axis, [(src, (src + shift) % count) for src in range(c...  35.6 us
    select_n x3, other arithmetic, gather_by_bits(): grown = jnp.where(here & reach == 0, mine_first, theirs_first)  35.2 us
    dot_general x4, matrix products, exchange_reduce(): jnp.dot(block_rows, weight, preferred_element_type=jnp.float32)  25.5 us
    dot_general x3, matrix products, absorb(): jnp.einsum('hqk,hkd->hqd', weights.astype(jnp.bfloat16), value_rows, pref...  21.8 us
    all_gather x1, waiting for transfers between devices, shards(): out_full = lax.all_gather(out_weight, 'req', axis=2, tiled=True)  21.8 us
    dot_general x1, matrix products, shards(): jnp.einsum('tc,ecn->ten', normed, query_full, preferred_element_type=jnp....  11.9 us
  transfers between devices with their start and end apart: 8, of which 7 were waited for; matrix products, arithmetic and copies ran while one was open for 22% of the time, Pallas kernels for 0%

profile of v1, /device:TPU:9, one launch (start us, length us, event | category | flops | bytes accessed | tf_op | source)
XLA Modules:
  0.0 530.3 jit_solution(4950938877877679058)
XLA Ops:
  8.0 4.0 collective-permute-done
  12.0 4.8 maximum_select_fusion.2
  18.0 90.9 %collective-permute-done.1 = bf16[8,512,512]{2,1,0:T(8,128)(2,1)} collective-permute-done((bf16[8,512,512]{2,1,0:T(8,128)(2,1)}, bf16[8,512,512]{2,1,0:T(8,128)(2,1)}, u32[]{:S(2)}, u32[]{:S(2)}) %collective-permute-start.1) | collective-permute-done | bytes 4194336 | tf_op jit(solution)/shard_map/ppermute | solution.py:15
  108.9 10.9 %maximum_select_fusion.1 = bf16[8,1024,512]{2,1,0:T(8,128)(2,1)} fusion(bf16[8,512,512]{2,1,0:T(8,128)(2,1)} %collective-permute-done.1, bf16[8,512,512]{2,1,0:T(8,128)(2,1)} %maximum_select_fusion.2, pred[]{:T(512)S(6)} %eq.45), kind=kLoop, calls=%fused_computation.27 | loop fusion | flops 37748736 | bytes 16777216 | tf_op jit(solution)/shard_map/jit(_where)/select_n | solution.py:18
  121.0 179.8 %collective-permute-done.2 = bf16[8,1024,512]{2,1,0:T(8,128)(2,1)} collective-permute-done((bf16[8,1024,512]{2,1,0:T(8,128)(2,1)}, bf16[8,1024,512]{2,1,0:T(8,128)(2,1)}, u32[]{:S(2)}, u32[]{:S(2)}) %collective-permute-start.2) | collective-permute-done | bytes 8388640 | tf_op jit(solution)/shard_map/ppermute | solution.py:15
  300.8 19.6 %maximum_select_fusion = bf16[8,2048,512]{2,1,0:T(8,128)(2,1)} fusion(bf16[8,1024,512]{2,1,0:T(8,128)(2,1)} %collective-permute-done.2, bf16[8,1024,512]{2,1,0:T(8,128)(2,1)} %maximum_select_fusion.1, pred[]{:T(512)S(6)} %eq.44), kind=kLoop, calls=%fused_computation.25 | loop fusion | flops 75497472 | bytes 33554432 | tf_op jit(solution)/shard_map/jit(_where)/select_n | solution.py:18
  332.3 11.9 %fusion.31 = f32[512,8,512]{2,0,1:T(8,128)S(1)} fusion(bf16[8,2048,512]{2,1,0:T(8,128)(2,1)} %maximum_select_fusion, bf16[512,2048]{1,0:T(8,128)(2,1)S(1)} %copy-done.8, f32[2048]{0:T(1024)S(1)} %copy-done.14, f32[512]{0:T(512)S(1)} %add_rsqrt_fusion), kind=kOutput, calls=%fused_computation.47 | convolution fusion | flops 8594128896 | bytes 27273216 | tf_op jit(solution)/shard_map/tc,ecn->ten/dot_general | solution.py:171
  344.2 4.9 copy.40
  349.0 8.2 %select_reduce_fusion = f32[512,2,512]{2,1,0:T(2,128)} fusion(f32[512,8,512]{2,1,0:T(8,128)S(1)} %copy.40, pred[512,2,8]{2,1,0:T(4,128)(4,1)S(1)} %copy.38), kind=kLoop, calls=%fused_computation.26 | loop fusion | flops 7864320 | bytes 10493952 | tf_op jit(solution)/shard_map/reduce_sum | solution.py:180
  357.3 3.3 reshape.253
  363.6 31.3 %while.14 = (s32[]{:T(128)}, f32[4,1024]{1,0:T(4,128)S(1)}, f32[4,1024]{1,0:T(4,128)S(1)}, f32[4,1024,128]{2,1,0:T(8,128)}, s32[]{:T(128)}, /*index=5*/s32[]{:T(...) while((s32[]{:T(128)}, f32[4,1024]{1,0:T(4,128)S(1)}, ...), condition=%wide.region_7.8_spmd, body=%wide.region_4.7_spmd.sunk | while | flops 1102063616 | bytes 65276644 | solution.py:89
  364.4 2.4 bitcast_reduce_fusion.2
  366.9 2.5 fusion.82
  370.7 9.3 %multiply_add_fusion.6 = f32[4,1024,128]{2,1,0:T(8,128)} fusion(f32[4,1024,128]{2,1,0:T(8,128)} %get-tuple-element.164, f32[4,512,1024]{2,1,0:T(8,128)} %copy-done.2, f32[4,1024]{1,0:T(4,128)S(1)} %max.8, pred[512]{0:T(512)(128)(4,1)S(1)} %fusion.81, f32[4,1024]{1,0:T(4,128)S(1)} %get-tuple-element.147, ...), kind=kOutput, calls=%fused_computation.10.clone.1 | convolution fusion | flops 548405248 | bytes 13141000 | tf_op jit(solution)/shard_map/while/body/hqk,hkd->hqd/dot_general | solution.py:70
  380.7 2.4 bitcast_reduce_fusion.2
  383.1 2.5 fusion.82
  386.3 8.5 %multiply_add_fusion.6 = f32[4,1024,128]{2,1,0:T(8,128)} fusion(f32[4,1024,128]{2,1,0:T(8,128)} %get-tuple-element.164, f32[4,512,1024]{2,1,0:T(8,128)} %copy-done.2, f32[4,1024]{1,0:T(4,128)S(1)} %max.8, pred[512]{0:T(512)(128)(4,1)S(1)} %fusion.81, f32[4,1024]{1,0:T(4,128)S(1)} %get-tuple-element.147, ...), kind=kOutput, calls=%fused_computation.10.clone.1 | convolution fusion | flops 548405248 | bytes 13141000 | tf_op jit(solution)/shard_map/while/body/hqk,hkd->hqd/dot_general | solution.py:70
  394.9 5.9 %fusion.59 = f32[512,1024]{1,0:T(8,128)} fusion(bf16[2048,1024]{1,0:T(8,128)(2,1)} %all-gather.3.cloned.1.call-done, bf16[512,2048]{1,0:T(8,128)(2,1)S(1)} %copy-done.9, f32[2048]{0:T(1024)S(1)} %copy-done.14, f32[512]{0:T(512)S(1)} %add_rsqrt_fusion), kind=kOutput, calls=%fused_computation.104 | convolution fusion | flops 2151677952 | bytes 8398848 | tf_op jit(solution)/shard_map/dot_general | solution.py:170
  400.7 3.4 reshape.254
  410.7 4.0 divide_bitcast_fusion
  414.7 2.7 copy.45
  417.4 3.0 reshape.255
  422.2 7.2 %select_reduce_fusion.1 = bf16[512,8,512]{2,1,0:T(8,128)(2,1)S(1)} fusion(pred[512,2,8]{2,1,0:T(4,128)(4,1)S(1)} %copy.38, bf16[512,2,512]{2,1,0:T(2,128)(2,1)S(1)} %multiply_convert_fusion), kind=kLoop, calls=%fused_computation.28 | loop fusion | flops 6291456 | bytes 5251072 | tf_op jit(solution)/shard_map/reduce_sum | solution.py:209
  429.4 4.2 copy.50
  433.6 21.8 %all-gather.5.cloned.1.call-done = bf16[8,512,2048]{2,1,0:T(8,128)(2,1)} async-done(((bf16[8,512,256]{2,1,0:T(8,128)(2,1)}), bf16[8,512,2048]{2,1,0:T(8,128)(2,1)}) %all-gather.5.cloned.1.call-update) | async-done | bytes 16777232 | tf_op jit(solution)/shard_map/all_gather | solution.py:169
  455.4 9.4 %convolution_convert_fusion.3 = bf16[128,2048]{1,0:T(8,128)(2,1)} fusion(bf16[4096,2048]{1,0:T(8,128)(2,1)} %bitcast.59, bf16[512,4096]{1,0:T(8,128)(2,1)} %bitcast.65, s32[]{:T(128)S(6)} %select_n.102), kind=kOutput, calls=%fused_computation.46 | convolution fusion | flops 2147745792 | bytes 18350084 | tf_op jit(solution)/shard_map/dot_general | solution.py:137
  467.6 3.3 convolution_convert_fusion.2
  470.9 2.1 collective-permute-start.4
  473.0 3.3 convolution_convert_fusion.1
  478.4 32.8 %collective-permute-done.4 = bf16[128,2048]{1,0:T(8,128)(2,1)} collective-permute-done((bf16[128,2048]{1,0:T(8,128)(2,1)}, bf16[128,2048]{1,0:T(8,128)(2,1)}, u32[]{:S(2)}, u32[]{:S(2)}) %collective-permute-start.4) | collective-permute-done | bytes 524320 | tf_op jit(solution)/shard_map/ppermute | solution.py:139
  511.2 2.5 collective-permute-done.5
  513.7 9.5 %add_convert_fusion.1 = bf16[128,2048]{1,0:T(8,128)(2,1)} fusion(bf16[128,2048]{1,0:T(8,128)(2,1)} %collective-permute-done.5, bf16[128,2048]{1,0:T(8,128)(2,1)} %collective-permute-done.4, bf16[128,2048]{1,0:T(8,128)(2,1)S(1)} %collective-permute-done.3, bf16[4096,2048]{1,0:T(8,128)(2,1)} %bitcast.60, bf16[512,4096]{1,0:T(8,128)(2,1)} %bitcast.66, ...), kind=kOutput, calls=%fused_computation.59 | convolution fusion | flops 2149842944 | bytes 19922948 | tf_op jit(solution)/shard_map/dot_general | solution.py:137
  (89 shorter events, 34.1 us)
Async XLA Ops:
  7.2 317.4 %copy-start = (f32[2048,8]{0,1:T(8,128)S(1)}, f32[2048,8]{0,1:T(8,128)}, u32[]{:S(2)}) copy-start(f32[2048,8]{0,1:T(8,128)} %param.13) | copy-start | bytes 196612
  7.2 387.7 %all-gather.3.cloned.1.call-start = ((), (), s32[]{:S(2)}) async-start(), calls=%async_computation | async-start | bytes 4718592 | tf_op jit(solution)/shard_map/all_gather | solution.py:168
  7.2 4.7 collective-permute-start
  16.8 92.1 %collective-permute-start.1 = (bf16[8,512,512]{2,1,0:T(8,128)(2,1)}, bf16[8,512,512]{2,1,0:T(8,128)(2,1)}, u32[]{:S(2)}, u32[]{:S(2)}) collective-permute-start(bf16[8,512,512]{2,1,0:T(8,128)(2,1)} %maximum_select_fusion.2), channel_id=1, source_target_pairs={{0,8},{4,12},{8,0},{12,4},{16,24},{20,28},{24,16},{28,20},{1,9},{5... | collective-permute-start | bytes 12582920 | tf_op jit(solution)/shard_map/ppermute | solution.py:15
  119.7 181.1 %collective-permute-start.2 = (bf16[8,1024,512]{2,1,0:T(8,128)(2,1)}, bf16[8,1024,512]{2,1,0:T(8,128)(2,1)}, u32[]{:S(2)}, u32[]{:S(2)}) collective-permute-start(bf16[8,1024,512]{2,1,0:T(8,128)(2,1)} %maximum_select_fusion.1), channel_id=1, source_target_pairs={{0,16},{4,20},{8,24},{12,28},{16,0},{20,4},{24,8},{28,12},{1,17},{... | collective-permute-start | bytes 25165832 | tf_op jit(solution)/shard_map/ppermute | solution.py:15
  121.0 200.2 %copy-start.15 = (s32[8]{0:T(128)S(1)}, s32[8]{0:T(128)}, u32[]{:S(2)}) copy-start(s32[8]{0:T(128)} %param.18) | copy-start | bytes 100
  121.0 201.6 %copy-start.13 = (s32[512,2]{0,1:T(2,128)S(1)}, s32[512,2]{0,1:T(2,128)}, u32[]{:S(2)}) copy-start(s32[512,2]{0,1:T(2,128)} %param.17) | copy-start | bytes 12292
  320.4 3.7 copy-start.8
  320.4 4.2 copy-start.14
  320.4 135.0 %all-gather.5.cloned.1.call-start = ((), (), s32[]{:S(2)}) async-start(), calls=%async_computation.1 | async-start | bytes 18874368 | tf_op jit(solution)/shard_map/all_gather | solution.py:169
  363.6 31.3 %copy-start.9 = (bf16[512,2048]{1,0:T(8,128)(2,1)S(1)}, bf16[512,2048]{1,0:T(8,128)(2,1)}, u32[]{:S(2)}) copy-start(bf16[512,2048]{1,0:T(8,128)(2,1)} %param.11) | copy-start | bytes 6291460
  366.9 3.8 copy-start.2
  383.1 3.2 copy-start.2
  404.2 1.9 copy-start.11
  404.2 1.9 copy-start.12
  404.9 1.7 copy-start.5
  406.0 4.7 copy-start.6
  408.5 2.2 copy-start.10
  455.4 11.0 %copy-start.3 = (bf16[8,512,2048]{2,1,0:T(8,128)(2,1)S(1)}, bf16[8,512,2048]{2,1,0:T(8,128)(2,1)}, u32[]{:S(2)}) copy-start(bf16[8,512,2048]{2,1,0:T(8,128)(2,1)} %all-gather.5.cloned.1.call-done) | copy-start | bytes 50331652
  455.4 12.2 %copy-start.4 = (bf16[64,8,8,512]{3,1,2,0:T(8,128)(2,1)S(1)}, bf16[64,8,8,512]{3,1,2,0:T(8,128)(2,1)}, u32[]{:S(2)}) copy-start(bf16[64,8,8,512]{3,1,2,0:T(8,128)(2,1)} %copy.50) | copy-start | bytes 12582916
  464.7 13.7 %collective-permute-start.3 = (bf16[128,2048]{1,0:T(8,128)(2,1)}, bf16[128,2048]{1,0:T(8,128)(2,1)S(1)}, u32[]{:S(2)}, u32[]{:S(2)}) collective-permute-start(bf16[128,2048]{1,0:T(8,128)(2,1)} %convolution_convert_fusion.3), channel_id=1, source_target_pairs={{0,1},{1,2},{2,3},{3,0},{4,5},{5,6},{6,7},{7,4},{8,9},{9,10},{10,1... | collective-permute-start | bytes 1572872 | tf_op jit(solution)/shard_map/ppermute | solution.py:139
  470.9 5.7 %copy-start.7 = (bf16[512,4,1,128]{3,2,1,0:T(2,128)(2,1)S(1)}, bf16[512,4,1,128]{3,2,1,0:T(2,128)(2,1)}, u32[]{:S(2)}) copy-start(bf16[512,4,1,128]{3,2,1,0:T(2,128)(2,1)} %copy-done.6) | copy-start | bytes 1572868
  470.9 40.3 %collective-permute-start.4 = (bf16[128,2048]{1,0:T(8,128)(2,1)}, bf16[128,2048]{1,0:T(8,128)(2,1)}, u32[]{:S(2)}, u32[]{:S(2)}) collective-permute-start(bf16[128,2048]{1,0:T(8,128)(2,1)} %convolution_convert_fusion.2), channel_id=1, source_target_pairs={{0,2},{1,3},{2,0},{3,1},{4,6},{5,7},{6,4},{7,5},{8,10},{9,11},{10,... | collective-permute-start | bytes 1572872 | tf_op jit(solution)/shard_map/ppermute | solution.py:139
  476.3 37.4 %collective-permute-start.5 = (bf16[128,2048]{1,0:T(8,128)(2,1)}, bf16[128,2048]{1,0:T(8,128)(2,1)}, u32[]{:S(2)}, u32[]{:S(2)}) collective-permute-start(bf16[128,2048]{1,0:T(8,128)(2,1)} %convolution_convert_fusion.1), channel_id=1, source_target_pairs={{0,3},{1,0},{2,1},{3,2},{4,7},{5,4},{6,5},{7,6},{8,11},{9,8},{10,9... | collective-permute-start | bytes 1572872 | tf_op jit(solution)/shard_map/ppermute | solution.py:139
  513.7 9.5 %copy-start.1 = (f32[2048,8]{0,1:T(8,128)S(1)}, f32[2048,8]{0,1:T(8,128)}, u32[]{:S(2)}) copy-start(f32[2048,8]{0,1:T(8,128)} %param.13) | copy-start | bytes 196612
Sparse Core Ops, SparseCore 0:
  320.5 39.7 all-gather.2
  362.2 93.1 all-gather.4
